TPU v7x, 128 devices: a whole 4x4x4 slice. The times are simulated.
128 devices in a mesh: seq: 16 (over z, x), heads: 8 (over y, core).
Axes of the slice: x: 4, y: 4, z: 4, core: 2. Of those that a mesh axis runs over, the one named last changes fastest.
Arguments:
- audio: bfloat16 [4096, 1280], P('seq'), may hold values from -6 to 6
- ln_gain: float32 [1280], replicated, may hold values from 0.25 to 1.75
- ln_shift: float32 [1280], replicated, may hold values from -3 to 3
- enc_wq: bfloat16 [1280, 1024], P(None, 'heads'), may hold values from -0.15625 to 0.15625
- enc_bq: float32 [1024], P('heads'), may hold values from -3 to 3
- enc_wk: bfloat16 [1280, 1024], P(None, 'heads'), may hold values from -4 to 4
- enc_wv: bfloat16 [1280, 1024], P(None, 'heads'), may hold values from -0.15625 to 0.15625
- enc_bv: float32 [1024], P('heads'), may hold values from -3 to 3
- enc_wo: bfloat16 [1024, 1280], P('heads'), may hold values from -0.1875 to 0.1875
- enc_bo: float32 [1280], replicated, may hold values from -3 to 3
- windows: int32 [16], P('heads'), may hold values from 1 to 128, as said below
- dec_wkv: bfloat16 [1280, 8, 256], replicated, may hold values from -4 to 4
- dec_bv: float32 [8, 128], replicated, may hold values from -3 to 3
- text: bfloat16 [8192, 8192], P('seq'), may hold values from -6 to 6
- norm_gain: float32 [8192], replicated, may hold values from 0.25 to 1.75
- dec_wq: bfloat16 [8192, 4096], P('seq', 'heads'), may hold values from -0.0625 to 0.0625
- dec_bq: float32 [4096], P('heads'), may hold values from -3 to 3
- dec_wo: bfloat16 [4096, 8192], P('heads', 'seq'), may hold values from -0.125 to 0.125
- span_start: int32 [8192], P('seq'), may hold values from 0 to 3840, as said below
- span_len: int32 [8192], P('seq'), may hold values from 1 to 256, as said below
Outputs:
- enc_out: bfloat16 [4096, 1280], P(('seq', 'heads'))
- dec_out: bfloat16 [8192, 8192], P('seq', 'heads')
Inputs may be any that keep to these rules, and one draw needn't show every extreme that they name: `windows`: every head's window is 1 to 128; some head has exactly 128 and some head exactly 1. `span_start`: row r's band begins between r * 256 // 512 - 255 and r * 256 // 512, and never before frame 0 or after 4096 - 256; row 0 begins at 0 and the last row at 3840; the last row of every aligned block of 512 rows but the final one begins exactly at r * 256 // 512. `span_len`: row 0 has 256 valid frames and row 1 has one; the last row of every aligned block of 512 rows has 256, unless it is row 1.
All inputs are finite; a program needn't handle non-finite values.
Results may differ from a plain program's by a relative error of at most 0.025.
Values may be sent and summed in bfloat16 or wider, within the bound.
No kernel may reach another device: no remote copies, remote signals or barrier semaphores. Data moves between devices by JAX's collectives and lax.ppermute only.
A program may use at most 128 MiB of HBM per device.

v0:
```python
import jax
import jax.numpy as jnp
from jax import lax
from jax.sharding import PartitionSpec as P

EWIN = 128
BAND = 256


def with_halo(block, sides, width):
    for axis, dim in sides:
        count = lax.axis_size(axis)
        forward = [(i, i + 1) for i in range(count - 1)]
        backward = [(target, source) for source, target in forward]
        low = lax.ppermute(
            lax.slice_in_dim(block, block.shape[dim] - width, None, axis=dim), axis, forward
        )
        high = lax.ppermute(lax.slice_in_dim(block, 0, width, axis=dim), axis, backward)
        block = jnp.concatenate([low, block, high], axis=dim)
    return block


def heads_gather(block, axis):
    count = lax.axis_size(axis)
    index = lax.axis_index(axis)
    gathered = block[None]
    bit = 1
    while bit < count:
        other = lax.ppermute(gathered, axis, [(i, i ^ bit) for i in range(count)])
        upper = index & bit != 0
        gathered = jnp.where(
            upper,
            jnp.concatenate([other, gathered], axis=0),
            jnp.concatenate([gathered, other], axis=0),
        )
        bit *= 2
    return gathered


def heads_ring_gather(block, axis):
    count = lax.axis_size(axis)
    ring = count // 2
    index = lax.axis_index(axis)
    chip = index // 2
    core = index % 2
    swap = [(i, i ^ 1) for i in range(count)]
    sibling = lax.ppermute(block, axis, swap)
    own = jnp.where(core == 0, jnp.stack([block, sibling]), jnp.stack([sibling, block]))
    step = []
    for i in range(count):
        direction = 1 if i % 2 == 0 else -1
        step.append((i, (i // 2 + direction) % ring * 2 + i % 2))
    near = lax.ppermute(own, axis, step)
    far = lax.ppermute(near, axis, step)
    other = lax.ppermute(near, axis, swap)
    sign = 1 - 2 * core
    owners = [chip, (chip - sign) % ring, (chip + 2) % ring, (chip + sign) % ring]
    return ([own, near, far, other], owners)


def layer_norm(values, gain, shift):
    values = values.astype(jnp.float32)
    centre = values - jnp.mean(values, axis=-1, keepdims=True)
    spread = jnp.mean(centre * centre, axis=-1, keepdims=True)
    return centre * lax.rsqrt(spread + 1e-05) * gain + shift


def rms_norm(values, gain):
    values = values.astype(jnp.float32)
    return values * lax.rsqrt(jnp.mean(values * values, axis=-1, keepdims=True) + 1e-06) * gain


def masked_softmax(scores, valid):
    highest = jnp.max(jnp.where(valid, scores, -jnp.inf), axis=-1, keepdims=True)
    raised = jnp.where(valid, jnp.exp(scores - highest), jnp.zeros_like(scores))
    return (raised / jnp.sum(raised, axis=-1, keepdims=True)).astype(jnp.bfloat16)


def shards(
    audio,
    ln_gain,
    ln_shift,
    enc_wq,
    enc_bq,
    enc_wk,
    enc_wv,
    enc_bv,
    enc_wo,
    enc_bo,
    windows,
    dec_wkv,
    dec_bv,
    text,
    norm_gain,
    dec_wq,
    dec_bq,
    dec_wo,
    span_start,
    span_len,
):
    seq_count = lax.axis_size("seq")
    head_count = lax.axis_size("heads")
    seq_index = lax.axis_index("seq")
    head_index = lax.axis_index("heads")
    frames_dev = audio.shape[0]
    enc_width = audio.shape[1]
    heads_dev = windows.shape[0]
    head_size = enc_wq.shape[1] // heads_dev
    all_frames = frames_dev * seq_count
    hidden = layer_norm(audio, ln_gain, ln_shift).astype(jnp.bfloat16)
    enc_query = (jnp.dot(hidden, enc_wq, preferred_element_type=jnp.float32) + enc_bq).astype(
        jnp.bfloat16
    )
    enc_keys = jnp.dot(hidden, enc_wk, preferred_element_type=jnp.float32).astype(jnp.bfloat16)
    enc_values = (jnp.dot(hidden, enc_wv, preferred_element_type=jnp.float32) + enc_bv).astype(
        jnp.bfloat16
    )
    enc_pairs = jnp.stack([enc_keys, enc_values], axis=1)
    widened = with_halo(enc_pairs, (("seq", 0),), EWIN)
    extent = frames_dev + 2 * EWIN
    key_block = widened[:, 0, :].reshape(extent, heads_dev, head_size)
    value_block = widened[:, 1, :].reshape(extent, heads_dev, head_size)
    query_block = enc_query.reshape(frames_dev, heads_dev, head_size)
    scores = jnp.einsum(
        "qhd,khd->hqk", query_block, key_block, preferred_element_type=jnp.float32
    ) * head_size ** (-0.5)
    row_frames = seq_index * frames_dev + jnp.arange(frames_dev, dtype=jnp.int32)
    col_frames = seq_index * frames_dev - EWIN + jnp.arange(extent, dtype=jnp.int32)
    distance = jnp.abs(row_frames[:, None] - col_frames[None, :])
    inside = (col_frames >= 0) & (col_frames < all_frames)
    valid = (distance[None, :, :] <= windows[:, None, None]) & inside[None, None, :]
    enc_weights = masked_softmax(scores, valid)
    enc_context = jnp.einsum(
        "hqk,khd->qhd", enc_weights, value_block, preferred_element_type=jnp.float32
    )
    enc_context = enc_context.astype(jnp.bfloat16).reshape(frames_dev, heads_dev * head_size)
    share = frames_dev // head_count
    enc_term = jnp.dot(enc_context, enc_wo, preferred_element_type=jnp.float32)
    mixed = jnp.sum(
        lax.all_to_all(
            enc_term.astype(jnp.bfloat16).reshape(head_count, share, enc_width),
            "heads",
            0,
            0,
            tiled=True,
        ).astype(jnp.float32),
        axis=0,
    )
    own_audio = lax.dynamic_slice_in_dim(audio, head_index * share, share, 0)
    enc_out = (own_audio.astype(jnp.float32) + mixed + enc_bo).astype(jnp.bfloat16)
    groups = dec_wkv.shape[1]
    groups_dev = groups // head_count
    pair_width = dec_wkv.shape[2]
    dec_head = pair_width // 2
    band_bias = jnp.concatenate([jnp.zeros_like(dec_bv), dec_bv], axis=1)
    share_pairs = (
        jnp.dot(
            enc_out,
            dec_wkv.reshape(enc_width, groups * pair_width),
            preferred_element_type=jnp.float32,
        )
        + band_bias.reshape(groups * pair_width)
    ).astype(jnp.bfloat16)
    band_pairs = lax.all_to_all(share_pairs, "heads", 1, 0, tiled=True)
    band_pairs = band_pairs.reshape(frames_dev, groups_dev, pair_width)
    band_wide = with_halo(band_pairs, (("seq", 0),), BAND)
    rows_dev = text.shape[0]
    model_width = text.shape[1]
    query_width = dec_wq.shape[1]
    query_heads = query_width // (groups_dev * dec_head)
    normed = rms_norm(text, norm_gain).astype(jnp.bfloat16)
    query_sum = jnp.dot(
        normed,
        lax.all_gather(dec_wq, "seq", axis=0, tiled=True),
        preferred_element_type=jnp.float32,
    )
    dec_query = (
        (query_sum + dec_bq)
        .astype(jnp.bfloat16)
        .reshape(rows_dev, groups_dev, query_heads, dec_head)
    )
    band_extent = band_wide.shape[0]
    band_keys = band_wide[:, :, :dec_head]
    band_values = band_wide[:, :, dec_head:]
    dec_scores = jnp.einsum(
        "rgqd,kgd->rgqk", dec_query, band_keys, preferred_element_type=jnp.float32
    ) * dec_head ** (-0.5)
    band_frames = seq_index * frames_dev - BAND + jnp.arange(band_extent, dtype=jnp.int32)
    in_band = (band_frames[None, :] >= span_start[:, None]) & (
        band_frames[None, :] < (span_start + span_len)[:, None]
    )
    dec_weights = masked_softmax(dec_scores, in_band[:, None, None, :])
    dec_context = jnp.einsum(
        "rgqk,kgd->rgqd", dec_weights, band_values, preferred_element_type=jnp.float32
    )
    dec_context = dec_context.astype(jnp.bfloat16).reshape(rows_dev, query_width)
    ratio = seq_count // head_count
    set_rows = dec_wo.shape[0]
    block_cols = dec_wo.shape[1]
    flat = [(c, j) for c in range(seq_count) for j in range(head_count)]
    regroup = [
        (c * head_count + j, (ratio * j + c % ratio) * head_count + c // ratio) for c, j in flat
    ]
    piece = lax.ppermute(dec_wo, ("seq", "heads"), regroup)
    pieces, owners = heads_ring_gather(dec_context, "heads")
    set_cols = ratio * block_cols
    column_weight = lax.all_gather(piece, "seq", axis=1, tiled=True)
    total = jnp.zeros((rows_dev, set_cols), jnp.float32)
    for held, owner in zip(pieces, owners):
        for offset in range(held.shape[0]):
            weight_set = lax.dynamic_slice_in_dim(
                column_weight, (owner * held.shape[0] + offset) * set_cols, set_cols, 1
            )
            term = jnp.dot(held[offset], weight_set, preferred_element_type=jnp.float32)
            total = total + term.astype(jnp.bfloat16).astype(jnp.float32)
    summed = total
    col_share = model_width // head_count
    own_text = lax.dynamic_slice_in_dim(text, head_index * col_share, col_share, 1)
    dec_out = (own_text.astype(jnp.float32) + summed).astype(jnp.bfloat16)
    return (enc_out, dec_out)


def solution(mesh):
    return jax.shard_map(
        shards,
        mesh=mesh,
        in_specs=(
            P("seq", None),
            P(),
            P(),
            P(None, "heads"),
            P("heads"),
            P(None, "heads"),
            P(None, "heads"),
            P("heads"),
            P("heads", None),
            P(),
            P("heads"),
            P(),
            P(),
            P("seq", None),
            P(),
            P("seq", "heads"),
            P("heads"),
            P("heads", "seq"),
            P("seq"),
            P("seq"),
        ),
        out_specs=(P(("seq", "heads"), None), P("seq", "heads")),
        check_vma=False,
    )
```

profile of v0, /device:TPU:1, one launch (start us, length us, event | category | flops | bytes accessed | tf_op | source)
XLA Modules:
  0.0 194.4 jit_solution(3535932592329753961)
XLA Ops:
  7.2 0.7 all-gather.3.cloned.1.call-update
  8.0 6.0 %collective-permute-start.5 = (bf16[512,512]{1,0:T(8,128)(2,1)}, bf16[512,512]{1,0:T(8,128)(2,1)S(1)}, u32[]{:S(2)}, u32[]{:S(2)}) collective-permute-start(bf16[512,512]{1,0:T(8,128)(2,1)} %param.37), channel_id=1, source_target_pairs={{0,0},{1,16},{2,32},{3,48},{4,64},{5,80},{6,96},{7,112},{8,8},{9,2... | collective-permute-start | bytes 1572872 | tf_op jit(solution)/shard_map/ppermute | solution.py:204
  14.0 7.1 %collective-permute-done.5 = bf16[512,512]{1,0:T(8,128)(2,1)S(1)} collective-permute-done((bf16[512,512]{1,0:T(8,128)(2,1)}, bf16[512,512]{1,0:T(8,128)(2,1)S(1)}, u32[]{:S(2)}, u32[]{:S(2)}) %collective-permute-start.5) | collective-permute-done | bytes 524320 | tf_op jit(solution)/shard_map/ppermute | solution.py:204
  21.1 0.8 copy-done.1
  21.9 1.3 convert_reduce_fusion
  23.2 1.5 fusion.25
  24.7 1.4 fusion.28
  26.1 1.3 fusion.40
  27.5 1.3 fusion.41
  28.8 3.1 %collective-permute-start = (bf16[128,2,128]{2,0,1:T(8,128)(2,1)S(1)}, bf16[128,2,128]{2,0,1:T(8,128)(2,1)S(1)}, u32[]{:S(2)}, u32[]{:S(2)}) collective-permute-start(bf16[128,2,128]{2,0,1:T(8,128)(2,1)S(1)} %get-tuple-element.4), channel_id=1, source_target_pairs={{0,8},{8,16},{16,24},{24,32},{32,40},{40,48},{48,56},{56,64},{64,7... | collective-permute-start | bytes 196616 | tf_op jit(solution)/shard_map/ppermute | solution.py:15
  31.9 1.3 collective-permute-start.1
  33.2 0.7 pad_bitcast_fusion
  33.9 7.1 %copy.45 = bf16[160,8,8,256]{3,1,2,0:T(8,128)(2,1)} copy(bf16[160,8,8,256]{3,2,1,0:T(8,128)(2,1)} %bitcast.108) | data formatting | bytes 10485760
  41.2 0.4 fusion.39
  42.3 0.7 fusion.75
  43.0 1.2 convolution_convert_fusion.9
  44.2 1.2 convolution_convert_fusion
  45.4 24.3 %all-to-all-start = ((bf16[8,32,1280]{2,1,0:T(8,128)(2,1)}), bf16[8,32,1280]{2,1,0:T(8,128)(2,1)S(1)}, u32[]{:S(2)}, u32[]{:S(2)}) async-start(bf16[8,32,1280]{2,1,0:T(8,128)(2,1)} %bitcast.7), calls=%async_computation | async-start | bytes 1310720 | tf_op jit(solution)/shard_map/all_to_all | solution.py:140
  69.8 5.3 %fusion.1 = f32[512]{0:T(512)S(1)} fusion(bf16[512,8192]{1,0:T(8,128)(2,1)} %param.33), kind=kLoop, calls=%fused_computation.3 | loop fusion | flops 12582400 | bytes 8390656 | tf_op jit(solution)/shard_map/reduce_sum | solution.py:70
  75.1 5.5 %all-to-all-done = bf16[8,32,1280]{2,1,0:T(8,128)(2,1)S(1)} async-done(((bf16[8,32,1280]{2,1,0:T(8,128)(2,1)}), bf16[8,32,1280]{2,1,0:T(8,128)(2,1)S(1)}, u32[]{:S(2)}, u32[]{:S(2)}) %all-to-all-start) | async-done | bytes 655392 | tf_op jit(solution)/shard_map/all_to_all | solution.py:140
  80.6 0.9 add_convert_fusion.1
  81.6 3.7 %fusion.14 = bf16[32,2048]{1,0:T(8,128)(2,1)S(1)} fusion(bf16[32,1280]{1,0:T(8,128)(2,1)S(1)} %add_convert_fusion.1, bf16[1280,2048]{1,0:T(8,128)(2,1)} %bitcast.107, f32[2048]{0:T(1024)S(1)} %bitcast.121), kind=kOutput, calls=%fused_computation.20 | convolution fusion | flops 167903232 | bytes 5464064 | tf_op jit(solution)/shard_map/dot_general | solution.py:157
  85.2 0.7 copy.48
  85.9 4.3 %all-to-all-start.1 = ((bf16[32,8,256]{2,0,1:T(8,128)(2,1)}), bf16[32,8,256]{2,0,1:T(8,128)(2,1)S(1)}, u32[]{:S(2)}, u32[]{:S(2)}) async-start(bf16[32,8,256]{2,0,1:T(8,128)(2,1)} %bitcast.106), calls=%async_computation.1 | async-start | bytes 262144 | tf_op jit(solution)/shard_map/all_to_all | solution.py:164
  90.5 4.9 %all-to-all-done.1 = bf16[32,8,256]{2,0,1:T(8,128)(2,1)S(1)} async-done(((bf16[32,8,256]{2,0,1:T(8,128)(2,1)}), bf16[32,8,256]{2,0,1:T(8,128)(2,1)S(1)}, u32[]{:S(2)}, u32[]{:S(2)}) %all-to-all-start.1) | async-done | bytes 131104 | tf_op jit(solution)/shard_map/all_to_all | solution.py:164
  95.4 1.3 collective-permute-start.3
  96.7 5.0 %collective-permute-start.2 = (bf16[256,1,256]{2,0,1:T(8,128)(2,1)S(1)}, bf16[256,1,256]{2,0,1:T(8,128)(2,1)S(1)}, u32[]{:S(2)}, u32[]{:S(2)}) collective-permute-start(bf16[256,1,256]{2,0,1:T(8,128)(2,1)S(1)} %bitcast.116), channel_id=1, source_target_pairs={{0,8},{8,16},{16,24},{24,32},{32,40},{40,48},{48,56},{56,64},{64,7... | collective-permute-start | bytes 393224 | tf_op jit(solution)/shard_map/ppermute | solution.py:15
  101.7 0.9 collective-permute-done.3
  102.6 0.9 collective-permute-done.2
  103.5 10.9 %fusion.35 = bf16[512,512]{0,1:T(8,128)(2,1)S(1)} fusion(bf16[8192,512]{1,0:T(8,128)(2,1)} %all-gather.3.cloned.1.call-done, bf16[512,8192]{1,0:T(8,128)(2,1)} %param.33, f32[8192]{0:T(1024)S(1)} %copy-done.9, f32[512]{0:T(512)S(1)} %add_rsqrt_fusion, f32[512]{0:T(512)S(1)} %copy-done.10), kind=kOutput, calls=%fused_computation.48 | convolution fusion | flops 4312268800 | bytes 17338368 | tf_op jit(solution)/shard_map/dot_general | solution.py:172
  114.5 1.2 fusion.8
  115.6 1.4 fusion.11
  117.0 2.1 %fusion.32 = bf16[128,512,4]{1,0,2:T(8,128)(2,1)S(1)} fusion(f32[512,4]{0,1:T(4,128)S(1)} %fusion.11, f32[512,4]{0,1:T(4,128)S(1)} %get-tuple-element.6, f32[768,512,4]{1,0,2:T(8,128)S(1)} %get-tuple-element.7, pred[512,768]{0,1:T(8,128)(4,1)S(1)} %compare_and_fusion, bf16[768,1,256]{2,0,1:T(8,128)(2,1)S(1)} %pad_maximum_fusion), kind=kOutput, calls=%fused_computation.47 | convolution fusion | flops 410779648 | bytes 7421952 | tf_op jit(solution)/shard_map/rgqk,kgd->rgqd/dot_general | solution.py:193
  119.1 1.9 collective-permute-start.4
  120.9 1.5 collective-permute-done.4
  122.7 0.9 collective-permute-start.6
  123.6 13.2 %collective-permute-done.6 = bf16[2,512,512]{1,2,0:T(8,128)(2,1)S(1)} collective-permute-done((bf16[2,512,512]{1,2,0:T(8,128)(2,1)S(1)}, bf16[2,512,512]{1,2,0:T(8,128)(2,1)S(1)}, u32[]{:S(2)}, u32[]{:S(2)}) %collective-permute-start.6) | collective-permute-done | bytes 1048608 | tf_op jit(solution)/shard_map/ppermute | solution.py:53
  136.8 2.1 %collective-permute-start.7 = (bf16[2,512,512]{1,2,0:T(8,128)(2,1)S(1)}, bf16[2,512,512]{1,2,0:T(8,128)(2,1)S(1)}, u32[]{:S(2)}, u32[]{:S(2)}) collective-permute-start(bf16[2,512,512]{1,2,0:T(8,128)(2,1)S(1)} %collective-permute-done.6), channel_id=1, source_target_pairs={{0,2},{1,7},{2,4},{3,1},{4,6},{5,3},{6,0},{7,5},{8,10},{9,15},{10,... | collective-permute-start | bytes 3145736 | tf_op jit(solution)/shard_map/ppermute | solution.py:54
  138.8 34.2 %all-gather.5.cloned.1.call-done = bf16[512,8192]{1,0:T(8,128)(2,1)} async-done(((bf16[512,512]{1,0:T(8,128)(2,1)}), bf16[512,8192]{1,0:T(8,128)(2,1)}) %all-gather.5.cloned.1.call-update) | async-done | bytes 8388624 | tf_op jit(solution)/shard_map/all_gather | solution.py:207
  173.1 2.1 %convolution_convert_fusion.7 = bf16[512,1024]{1,0:T(8,128)(2,1)S(1)} fusion(bf16[512,8192]{1,0:T(8,128)(2,1)} %all-gather.5.cloned.1.call-done, s32[]{:T(128)S(6)} %select_n.88, bf16[2,512,512]{1,2,0:T(8,128)(2,1)S(1)} %maximum_select_fusion), kind=kOutput, calls=%fused_computation.33 | convolution fusion | flops 537395200 | bytes 2621444 | tf_op jit(solution)/shard_map/dot_general | solution.py:214
  175.2 2.5 %convolution_convert_fusion.8 = bf16[512,1024]{1,0:T(8,128)(2,1)S(1)} fusion(bf16[512,8192]{1,0:T(8,128)(2,1)} %all-gather.5.cloned.1.call-done, s32[]{:T(128)S(6)} %select_n.87, bf16[2,512,512]{1,2,0:T(8,128)(2,1)S(1)} %maximum_select_fusion), kind=kOutput, calls=%fused_computation.34 | convolution fusion | flops 537395200 | bytes 2621444 | tf_op jit(solution)/shard_map/dot_general | solution.py:214
  177.7 2.3 %collective-permute-start.8 = (bf16[2,512,512]{1,2,0:T(8,128)(2,1)S(1)}, bf16[2,512,512]{1,2,0:T(8,128)(2,1)S(1)}, u32[]{:S(2)}, u32[]{:S(2)}) collective-permute-start(bf16[2,512,512]{1,2,0:T(8,128)(2,1)S(1)} %collective-permute-done.6), channel_id=1, source_target_pairs={{0,1},{1,0},{2,3},{3,2},{4,5},{5,4},{6,7},{7,6},{8,9},{9,8},{10,11... | collective-permute-start | bytes 3145736 | tf_op jit(solution)/shard_map/ppermute | solution.py:55
  180.0 0.7 convolution_convert_fusion.5
  180.7 0.7 convolution_convert_fusion.6
  181.5 0.7 convolution_convert_fusion.3
  182.3 0.7 convolution_convert_fusion.4
  183.0 0.7 convolution_convert_fusion.2
  183.8 3.8 %add_convert_fusion = bf16[512,1024]{1,0:T(8,128)(2,1)} fusion(bf16[512,1024]{1,0:T(8,128)(2,1)S(1)} %convolution_convert_fusion.2, bf16[512,1024]{1,0:T(8,128)(2,1)S(1)} %convolution_convert_fusion.3, bf16[512,1024]{1,0:T(8,128)(2,1)S(1)} %convolution_convert_fusion.4, bf16[512,1024]{1,0:T(8,128)(2,1)S(1)} %convolution_convert_fusion.5, ...), kind=kOutput, calls=%fused_computation.21 | convolution fusion | flops 546832384 | bytes 11010056 | tf_op jit(solution)/shard_map/dot_general | solution.py:214
  (51 shorter events, 1.7 us)
Async XLA Ops:
  7.2 37.1 %copy-start = (bf16[128,1280]{1,0:T(8,128)(2,1)S(1)}, bf16[128,1280]{1,0:T(8,128)(2,1)}, u32[]{:S(2)}) copy-start(bf16[128,1280]{1,0:T(8,128)(2,1)} %param.28) | copy-start | bytes 983044
  7.2 96.3 %all-gather.3.cloned.1.call-start = ((), (), s32[]{:S(2)}) async-start(), calls=%async_computation.2 | async-start | bytes 8912896 | tf_op jit(solution)/shard_map/all_gather | solution.py:174
  7.9 165.2 %all-gather.5.cloned.1.call-start = ((), (), s32[]{:S(2)}) async-start(), calls=%async_computation.3 | async-start | bytes 8912896 | tf_op jit(solution)/shard_map/all_gather | solution.py:207
  8.0 13.1 %collective-permute-start.5 = (bf16[512,512]{1,0:T(8,128)(2,1)}, bf16[512,512]{1,0:T(8,128)(2,1)S(1)}, u32[]{:S(2)}, u32[]{:S(2)}) collective-permute-start(bf16[512,512]{1,0:T(8,128)(2,1)} %param.37), channel_id=1, source_target_pairs={{0,0},{1,16},{2,32},{3,48},{4,64},{5,80},{6,96},{7,112},{8,8},{9,2... | collective-permute-start | bytes 1572872 | tf_op jit(solution)/shard_map/ppermute | solution.py:204
  21.1 0.8 copy-start.1
  26.1 14.9 %copy-start.4 = (s32[512]{0:T(512)S(1)}, s32[512]{0:T(512)}, u32[]{:S(2)}) copy-start(s32[512]{0:T(512)} %param.38) | copy-start | bytes 6148
  26.1 14.9 %copy-start.6 = (s32[512]{0:T(512)S(1)}, s32[512]{0:T(512)}, u32[]{:S(2)}) copy-start(s32[512]{0:T(512)} %param.39) | copy-start | bytes 6148
  27.4 13.8 %copy-start.2 = (bf16[1280,128]{1,0:T(8,128)(2,1)S(1)}, bf16[1280,128]{1,0:T(8,128)(2,1)}, u32[]{:S(2)}) copy-start(bf16[1280,128]{1,0:T(8,128)(2,1)} %param.23) | copy-start | bytes 983044
  27.4 13.8 %copy-start.7 = (f32[128]{0:T(128)S(1)}, f32[128]{0:T(128)}, u32[]{:S(2)}) copy-start(f32[128]{0:T(128)} %param.24) | copy-start | bytes 1540
  28.8 12.8 %collective-permute-start = (bf16[128,2,128]{2,0,1:T(8,128)(2,1)S(1)}, bf16[128,2,128]{2,0,1:T(8,128)(2,1)S(1)}, u32[]{:S(2)}, u32[]{:S(2)}) collective-permute-start(bf16[128,2,128]{2,0,1:T(8,128)(2,1)S(1)} %get-tuple-element.4), channel_id=1, source_target_pairs={{0,8},{8,16},{16,24},{24,32},{32,40},{40,48},{48,56},{56,64},{64,7... | collective-permute-start | bytes 196616 | tf_op jit(solution)/shard_map/ppermute | solution.py:15
  31.9 9.7 %collective-permute-start.1 = (bf16[128,2,128]{2,0,1:T(8,128)(2,1)S(1)}, bf16[128,2,128]{2,0,1:T(8,128)(2,1)S(1)}, u32[]{:S(2)}, u32[]{:S(2)}) collective-permute-start(bf16[128,2,128]{2,0,1:T(8,128)(2,1)S(1)} %get-tuple-element.5), channel_id=1, source_target_pairs={{8,0},{16,8},{24,16},{32,24},{40,32},{48,40},{56,48},{64,56},{72,6... | collective-permute-start | bytes 196616 | tf_op jit(solution)/shard_map/ppermute | solution.py:18
  33.9 8.4 %copy-start.11 = (s32[2]{0:T(128)S(1)}, s32[2]{0:T(128)}, u32[]{:S(2)}) copy-start(s32[2]{0:T(128)} %param.30) | copy-start | bytes 28
  44.2 36.4 %copy-start.5 = (f32[1280]{0:T(1024)S(1)}, f32[1280]{0:T(1024)}, u32[]{:S(2)}) copy-start(f32[1280]{0:T(1024)} %param.29) | copy-start | bytes 15364
  45.4 35.1 %all-to-all-start = ((bf16[8,32,1280]{2,1,0:T(8,128)(2,1)}), bf16[8,32,1280]{2,1,0:T(8,128)(2,1)S(1)}, u32[]{:S(2)}, u32[]{:S(2)}) async-start(bf16[8,32,1280]{2,1,0:T(8,128)(2,1)} %bitcast.7), calls=%async_computation | async-start | bytes 1310720 | tf_op jit(solution)/shard_map/all_to_all | solution.py:140
  69.8 33.7 %copy-start.9 = (f32[8192]{0:T(1024)S(1)}, f32[8192]{0:T(1024)}, u32[]{:S(2)}) copy-start(f32[8192]{0:T(1024)} %param.34) | copy-start | bytes 98308
  69.8 33.7 %copy-start.10 = (f32[512]{0:T(512)S(1)}, f32[512]{0:T(512)}, u32[]{:S(2)}) copy-start(f32[512]{0:T(512)} %param.36) | copy-start | bytes 6148
  81.6 32.9 %copy-start.3 = (bf16[32,1280]{1,0:T(8,128)(2,1)}, bf16[32,1280]{1,0:T(8,128)(2,1)S(1)}, u32[]{:S(2)}) copy-start(bf16[32,1280]{1,0:T(8,128)(2,1)S(1)} %add_convert_fusion.1) | copy-start | bytes 245764
  85.9 9.5 %all-to-all-start.1 = ((bf16[32,8,256]{2,0,1:T(8,128)(2,1)}), bf16[32,8,256]{2,0,1:T(8,128)(2,1)S(1)}, u32[]{:S(2)}, u32[]{:S(2)}) async-start(bf16[32,8,256]{2,0,1:T(8,128)(2,1)} %bitcast.106), calls=%async_computation.1 | async-start | bytes 262144 | tf_op jit(solution)/shard_map/all_to_all | solution.py:164
  95.4 7.2 %collective-permute-start.3 = (bf16[256,1,256]{2,0,1:T(8,128)(2,1)S(1)}, bf16[256,1,256]{2,0,1:T(8,128)(2,1)S(1)}, u32[]{:S(2)}, u32[]{:S(2)}) collective-permute-start(bf16[256,1,256]{2,0,1:T(8,128)(2,1)S(1)} %bitcast.115), channel_id=1, source_target_pairs={{8,0},{16,8},{24,16},{32,24},{40,32},{48,40},{56,48},{64,56},{72,6... | collective-permute-start | bytes 393224 | tf_op jit(solution)/shard_map/ppermute | solution.py:18
  96.7 6.7 %collective-permute-start.2 = (bf16[256,1,256]{2,0,1:T(8,128)(2,1)S(1)}, bf16[256,1,256]{2,0,1:T(8,128)(2,1)S(1)}, u32[]{:S(2)}, u32[]{:S(2)}) collective-permute-start(bf16[256,1,256]{2,0,1:T(8,128)(2,1)S(1)} %bitcast.116), channel_id=1, source_target_pairs={{0,8},{8,16},{16,24},{24,32},{32,40},{40,48},{48,56},{56,64},{64,7... | collective-permute-start | bytes 393224 | tf_op jit(solution)/shard_map/ppermute | solution.py:15
  119.1 3.4 %collective-permute-start.4 = (bf16[512,512]{0,1:T(8,128)(2,1)S(1)}, bf16[512,512]{0,1:T(8,128)(2,1)S(1)}, u32[]{:S(2)}, u32[]{:S(2)}) collective-permute-start(bf16[512,512]{0,1:T(8,128)(2,1)S(1)} %bitcast.109), channel_id=1, source_target_pairs={{0,1},{1,0},{2,3},{3,2},{4,5},{5,4},{6,7},{7,6},{8,9},{9,8},{10,11... | collective-permute-start | bytes 1572872 | tf_op jit(solution)/shard_map/ppermute | solution.py:47
  122.7 14.1 %collective-permute-start.6 = (bf16[2,512,512]{1,2,0:T(8,128)(2,1)S(1)}, bf16[2,512,512]{1,2,0:T(8,128)(2,1)S(1)}, u32[]{:S(2)}, u32[]{:S(2)}) collective-permute-start(bf16[2,512,512]{1,2,0:T(8,128)(2,1)S(1)} %maximum_select_fusion), channel_id=1, source_target_pairs={{0,2},{1,7},{2,4},{3,1},{4,6},{5,3},{6,0},{7,5},{8,10},{9,15},{10,... | collective-permute-start | bytes 3145736 | tf_op jit(solution)/shard_map/ppermute | solution.py:53
  136.8 44.7 %collective-permute-start.7 = (bf16[2,512,512]{1,2,0:T(8,128)(2,1)S(1)}, bf16[2,512,512]{1,2,0:T(8,128)(2,1)S(1)}, u32[]{:S(2)}, u32[]{:S(2)}) collective-permute-start(bf16[2,512,512]{1,2,0:T(8,128)(2,1)S(1)} %collective-permute-done.6), channel_id=1, source_target_pairs={{0,2},{1,7},{2,4},{3,1},{4,6},{5,3},{6,0},{7,5},{8,10},{9,15},{10,... | collective-permute-start | bytes 3145736 | tf_op jit(solution)/shard_map/ppermute | solution.py:54
  173.1 6.9 %copy-start.8 = (bf16[512,8192]{1,0:T(8,128)(2,1)S(1)}, bf16[512,8192]{1,0:T(8,128)(2,1)}, u32[]{:S(2)}) copy-start(bf16[512,8192]{1,0:T(8,128)(2,1)} %all-gather.5.cloned.1.call-done) | copy-start | bytes 25165828
  177.7 5.4 %collective-permute-start.8 = (bf16[2,512,512]{1,2,0:T(8,128)(2,1)S(1)}, bf16[2,512,512]{1,2,0:T(8,128)(2,1)S(1)}, u32[]{:S(2)}, u32[]{:S(2)}) collective-permute-start(bf16[2,512,512]{1,2,0:T(8,128)(2,1)S(1)} %collective-permute-done.6), channel_id=1, source_target_pairs={{0,1},{1,0},{2,3},{3,2},{4,5},{5,4},{6,7},{7,6},{8,9},{9,8},{10,11... | collective-permute-start | bytes 3145736 | tf_op jit(solution)/shard_map/ppermute | solution.py:55
Sparse Core Ops, SparseCore 0:
  10.1 85.0 all-gather.2
  97.3 75.7 all-gather.4
where the time goes:
time: 195 us; the launch traced here: 194 us
  waiting for transfers between devices  68.8 us (35%)
  starting transfers between devices  52.6 us (27%)
  matrix products  35.7 us (18%)
  between operations  14.5 us (7%)
  other arithmetic  13.3 us (7%)
  local copies, waits for them, and re-layouts  9.56 us (5%)
    all_gather x1, waiting for transfers between devices, shards(): column_weight = lax.all_gather(piece, 'seq', axis=1, tiled=True)  34.2 us
    all_to_all x1, starting transfers between devices, shards(): lax.all_to_all(enc_term.astype(jnp.bfloat16).reshape(head_count, share, e...  24.3 us
    ppermute x1, waiting for transfers between devices, heads_ring_gather(): near = lax.ppermute(own, axis, step)  13.2 us
    dot_general x8, matrix products, shards(): term = jnp.dot(held[offset], weight_set, preferred_element_type=jnp.float32)  12 us
    dot_general x1, matrix products, shards(): jnp.dot(normed, lax.all_gather(dec_wq, 'seq', axis=0, tiled=True), prefer...  10.9 us
    unnamed x27, local copies, waits for them, and re-layouts  8.65 us
    ppermute x2, starting transfers between devices, with_halo(): lax.ppermute(lax.slice_in_dim(block, block.shape[dim] - width, None, axis...  8.07 us
    ppermute x1, waiting for transfers between devices, shards(): piece = lax.ppermute(dec_wo, ('seq', 'heads'), regroup)  7.06 us
  transfers between devices with their start and end apart: 13, of which 8 were waited for; matrix products, arithmetic and copies ran while one was open for 27% of the time, Pallas kernels for 0%

commit v1 on v0

--- a/solution.py
+++ b/solution.py
@@ -204,7 +204,9 @@
     piece = lax.ppermute(dec_wo, ("seq", "heads"), regroup)
     pieces, owners = heads_ring_gather(dec_context, "heads")
     set_cols = ratio * block_cols
-    column_weight = lax.all_gather(piece, "seq", axis=1, tiled=True)
+    found_now = jnp.stack([piece for _ in range(jax.lax.axis_size("seq"))], 0)
+    vec_out = jax.lax.all_to_all(found_now, axis_name="seq", split_axis=0, concat_axis=0)
+    column_weight = jnp.concatenate(vec_out, 1)
     total = jnp.zeros((rows_dev, set_cols), jnp.float32)
     for held, owner in zip(pieces, owners):
         for offset in range(held.shape[0]):

time: 195 us -> 287 us (1.47)
  the two profiles are of different devices: /device:TPU:1 before, /device:TPU:118 now
where the time goes in v1:
time: 287 us; the launch traced here: 286 us
  waiting for transfers between devices  165 us (57%)
  matrix products  41.9 us (15%)
  starting transfers between devices  38.8 us (14%)
  between operations  14.6 us (5%)
  other arithmetic  13.1 us (5%)
  local copies, waits for them, and re-layouts  12.4 us (4%)
    ppermute x2, waiting for transfers between devices, with_halo(): lax.ppermute(lax.slice_in_dim(block, 0, width, axis=dim), axis, backward)  100 us
    ppermute x2, waiting for transfers between devices, with_halo(): lax.ppermute(lax.slice_in_dim(block, block.shape[dim] - width, None, axis...  31.6 us
    dot_general x8, matrix products, shards(): term = jnp.dot(held[offset], weight_set, preferred_element_type=jnp.float32)  18 us
    ppermute x1, waiting for transfers between devices, heads_ring_gather(): near = lax.ppermute(own, axis, step)  14.7 us
    all_to_all x1, starting transfers between devices, shards(): jax.lax.all_to_all(found_now, axis_name='seq', split_axis=0, concat_axis=0)  12.3 us
    dot_general x1, matrix products, shards(): jnp.dot(normed, lax.all_gather(dec_wq, 'seq', axis=0, tiled=True), prefer...  10.4 us
    all_to_all x1, starting transfers between devices, shards(): band_pairs = lax.all_to_all(share_pairs, 'heads', 1, 0, tiled=True)  9.55 us
    unnamed x25, local copies, waits for them, and re-layouts  7.23 us
  transfers between devices with their start and end apart: 13, of which 8 were waited for; matrix products, arithmetic and copies ran while one was open for 21% of the time, Pallas kernels for 0%

profile of v1, /device:TPU:118, one launch (start us, length us, event | category | flops | bytes accessed | tf_op | source)
XLA Modules:
  0.0 285.7 jit_solution(16833960740459727969)
XLA Ops:
  7.2 0.7 all-gather.2.cloned.1.call-update
  7.9 1.3 convert_reduce_fusion
  9.2 1.4 fusion.25
  10.6 1.4 fusion.28
  12.0 1.3 fusion.40
  13.3 1.3 fusion.41
  14.6 2.7 collective-permute-start.1
  17.4 1.3 collective-permute-start
  18.9 1.4 fusion.39
  20.3 3.7 %collective-permute-done = bf16[128,2,128]{2,0,1:T(8,128)(2,1)S(1)} collective-permute-done((bf16[128,2,128]{2,0,1:T(8,128)(2,1)S(1)}, bf16[128,2,128]{2,0,1:T(8,128)(2,1)S(1)}, u32[]{:S(2)}, u32[]{:S(2)}) %collective-permute-start) | collective-permute-done | bytes 65568 | tf_op jit(solution)/shard_map/ppermute | solution.py:15
  24.3 0.3 convolution_multiply_fusion
  24.6 0.7 fusion.75
  25.3 1.2 convolution_convert_fusion.9
  26.5 1.2 convolution_convert_fusion
  27.7 4.9 %all-to-all-start = ((bf16[8,32,1280]{2,1,0:T(8,128)(2,1)}), bf16[8,32,1280]{2,1,0:T(8,128)(2,1)S(1)}, u32[]{:S(2)}, u32[]{:S(2)}) async-start(bf16[8,32,1280]{2,1,0:T(8,128)(2,1)} %bitcast.7), calls=%async_computation | async-start | bytes 1310720 | tf_op jit(solution)/shard_map/all_to_all | solution.py:140
  32.6 3.2 %collective-permute-start.5 = (bf16[512,512]{1,0:T(8,128)(2,1)S(1)}, bf16[512,512]{1,0:T(8,128)(2,1)S(1)}, u32[]{:S(2)}, u32[]{:S(2)}) collective-permute-start(bf16[512,512]{1,0:T(8,128)(2,1)S(1)} %copy-done.7), channel_id=1, source_target_pairs={{0,0},{1,16},{2,32},{3,48},{4,64},{5,80},{6,96},{7,112},{8,8},{9,2... | collective-permute-start | bytes 1572872 | tf_op jit(solution)/shard_map/ppermute | solution.py:204
  35.9 7.2 %copy.47 = bf16[160,8,8,256]{3,1,2,0:T(8,128)(2,1)} copy(bf16[160,8,8,256]{3,2,1,0:T(8,128)(2,1)} %bitcast.111) | data formatting | bytes 10485760
  43.0 6.2 %all-to-all-done = bf16[8,32,1280]{2,1,0:T(8,128)(2,1)S(1)} async-done(((bf16[8,32,1280]{2,1,0:T(8,128)(2,1)}), bf16[8,32,1280]{2,1,0:T(8,128)(2,1)S(1)}, u32[]{:S(2)}, u32[]{:S(2)}) %all-to-all-start) | async-done | bytes 655392 | tf_op jit(solution)/shard_map/all_to_all | solution.py:140
  49.4 0.9 add_convert_fusion.1
  50.3 3.5 %fusion.14 = bf16[32,2048]{1,0:T(8,128)(2,1)S(1)} fusion(bf16[32,1280]{1,0:T(8,128)(2,1)S(1)} %add_convert_fusion.1, bf16[1280,2048]{1,0:T(8,128)(2,1)} %bitcast.110, f32[2048]{0:T(1024)S(1)} %bitcast.124), kind=kOutput, calls=%fused_computation.20 | convolution fusion | flops 167903232 | bytes 5464064 | tf_op jit(solution)/shard_map/dot_general | solution.py:157
  53.8 0.7 copy.50
  54.5 9.6 %all-to-all-start.1 = ((bf16[32,8,256]{2,0,1:T(8,128)(2,1)}), bf16[32,8,256]{2,0,1:T(8,128)(2,1)S(1)}, u32[]{:S(2)}, u32[]{:S(2)}) async-start(bf16[32,8,256]{2,0,1:T(8,128)(2,1)} %bitcast.109), calls=%async_computation.1 | async-start | bytes 262144 | tf_op jit(solution)/shard_map/all_to_all | solution.py:164
  64.1 0.2 copy.41
  64.3 3.2 %all-to-all-done.1 = bf16[32,8,256]{2,0,1:T(8,128)(2,1)S(1)} async-done(((bf16[32,8,256]{2,0,1:T(8,128)(2,1)}), bf16[32,8,256]{2,0,1:T(8,128)(2,1)S(1)}, u32[]{:S(2)}, u32[]{:S(2)}) %all-to-all-start.1) | async-done | bytes 131104 | tf_op jit(solution)/shard_map/all_to_all | solution.py:164
  67.4 4.0 %stack.20 = bf16[16,512,512]{1,2,0:T(8,128)(2,1)} broadcast(bf16[512,512]{0,1:T(8,128)(2,1)S(1)} %copy.41), dimensions={1,2} | broadcast | bytes 8912896 | tf_op jit(solution)/shard_map/stack | solution.py:207
  71.5 12.3 %all-to-all-start.2 = ((bf16[16,512,512]{1,2,0:T(8,128)(2,1)}), bf16[16,512,512]{1,2,0:T(8,128)(2,1)}, u32[]{:S(2)}, u32[]{:S(2)}) async-start(bf16[16,512,512]{1,2,0:T(8,128)(2,1)} %stack.20), calls=%async_computation.2 | async-start | bytes 16777216 | tf_op jit(solution)/shard_map/all_to_all | solution.py:208
  83.9 0.4 compare_and_fusion
  84.2 5.2 %fusion.1 = f32[512]{0:T(512)S(1)} fusion(bf16[512,8192]{1,0:T(8,128)(2,1)} %param.33), kind=kLoop, calls=%fused_computation.3 | loop fusion | flops 12582400 | bytes 8390656 | tf_op jit(solution)/shard_map/reduce_sum | solution.py:70
  89.5 2.8 collective-permute-start.3
  92.3 1.5 collective-permute-start.2
  93.8 100.2 %collective-permute-done.3 = bf16[256,1,256]{2,0,1:T(8,128)(2,1)S(1)} collective-permute-done((bf16[256,1,256]{2,0,1:T(8,128)(2,1)S(1)}, bf16[256,1,256]{2,0,1:T(8,128)(2,1)S(1)}, u32[]{:S(2)}, u32[]{:S(2)}) %collective-permute-start.3) | collective-permute-done | bytes 131104 | tf_op jit(solution)/shard_map/ppermute | solution.py:18
  193.9 27.9 %collective-permute-done.2 = bf16[256,1,256]{2,0,1:T(8,128)(2,1)S(1)} collective-permute-done((bf16[256,1,256]{2,0,1:T(8,128)(2,1)S(1)}, bf16[256,1,256]{2,0,1:T(8,128)(2,1)S(1)}, u32[]{:S(2)}, u32[]{:S(2)}) %collective-permute-start.2) | collective-permute-done | bytes 131104 | tf_op jit(solution)/shard_map/ppermute | solution.py:15
  221.9 10.4 %fusion.35 = bf16[512,512]{0,1:T(8,128)(2,1)S(1)} fusion(bf16[8192,512]{1,0:T(8,128)(2,1)} %all-gather.2.cloned.1.call-done, bf16[512,8192]{1,0:T(8,128)(2,1)} %param.33, f32[8192]{0:T(1024)S(1)} %copy-done.8, f32[512]{0:T(512)S(1)} %add_rsqrt_fusion, f32[512]{0:T(512)S(1)} %copy-done.9), kind=kOutput, calls=%fused_computation.48 | convolution fusion | flops 4312268800 | bytes 17338368 | tf_op jit(solution)/shard_map/dot_general | solution.py:172
  232.3 1.2 fusion.8
  233.5 1.4 fusion.11
  234.8 2.1 fusion.32
  237.0 1.9 collective-permute-done.4
  239.3 14.7 %collective-permute-done.6 = bf16[2,512,512]{1,2,0:T(8,128)(2,1)S(1)} collective-permute-done((bf16[2,512,512]{1,2,0:T(8,128)(2,1)S(1)}, bf16[2,512,512]{1,2,0:T(8,128)(2,1)S(1)}, u32[]{:S(2)}, u32[]{:S(2)}) %collective-permute-start.6) | collective-permute-done | bytes 1048608 | tf_op jit(solution)/shard_map/ppermute | solution.py:53
  254.0 2.0 convolution_convert_fusion.7
  256.0 2.0 convolution_convert_fusion.8
  258.0 0.3 collective-permute-start.8
  258.3 2.0 convolution_convert_fusion.5
  260.3 2.0 convolution_convert_fusion.6
  262.3 6.5 %collective-permute-done.7 = bf16[2,512,512]{1,2,0:T(8,128)(2,1)S(1)} collective-permute-done((bf16[2,512,512]{1,2,0:T(8,128)(2,1)S(1)}, bf16[2,512,512]{1,2,0:T(8,128)(2,1)S(1)}, u32[]{:S(2)}, u32[]{:S(2)}) %collective-permute-start.7) | collective-permute-done | bytes 1048608 | tf_op jit(solution)/shard_map/ppermute | solution.py:54
  268.8 2.0 convolution_convert_fusion.3
  270.8 2.0 convolution_convert_fusion.4
  272.8 2.0 convolution_convert_fusion.2
  274.8 4.1 %add_convert_fusion = bf16[512,1024]{1,0:T(8,128)(2,1)} fusion(bf16[512,1024]{1,0:T(8,128)(2,1)S(1)} %convolution_convert_fusion.2, bf16[512,1024]{1,0:T(8,128)(2,1)S(1)} %convolution_convert_fusion.3, bf16[512,1024]{1,0:T(8,128)(2,1)S(1)} %convolution_convert_fusion.4, bf16[512,1024]{1,0:T(8,128)(2,1)S(1)} %convolution_convert_fusion.5, ...), kind=kOutput, calls=%fused_computation.21 | convolution fusion | flops 546832384 | bytes 11010056 | tf_op jit(solution)/shard_map/dot_general | solution.py:216
  (50 shorter events, 1.1 us)
Async XLA Ops:
  7.2 19.3 %copy-start = (bf16[128,1280]{1,0:T(8,128)(2,1)S(1)}, bf16[128,1280]{1,0:T(8,128)(2,1)}, u32[]{:S(2)}) copy-start(bf16[128,1280]{1,0:T(8,128)(2,1)} %param.28) | copy-start | bytes 983044
  7.2 17.5 %copy-start.10 = (s32[2]{0:T(128)S(1)}, s32[2]{0:T(128)}, u32[]{:S(2)}) copy-start(s32[2]{0:T(128)} %param.30) | copy-start | bytes 28
  7.2 214.7 %all-gather.2.cloned.1.call-start = ((), (), s32[]{:S(2)}) async-start(), calls=%async_computation.3 | async-start | bytes 8912896 | tf_op jit(solution)/shard_map/all_gather | solution.py:174
  14.6 5.6 %collective-permute-start.1 = (bf16[128,2,128]{2,0,1:T(8,128)(2,1)S(1)}, bf16[128,2,128]{2,0,1:T(8,128)(2,1)S(1)}, u32[]{:S(2)}, u32[]{:S(2)}) collective-permute-start(bf16[128,2,128]{2,0,1:T(8,128)(2,1)S(1)} %get-tuple-element.5), channel_id=1, source_target_pairs={{8,0},{16,8},{24,16},{32,24},{40,32},{48,40},{56,48},{64,56},{72,6... | collective-permute-start | bytes 196616 | tf_op jit(solution)/shard_map/ppermute | solution.py:18
  17.4 6.6 %collective-permute-start = (bf16[128,2,128]{2,0,1:T(8,128)(2,1)S(1)}, bf16[128,2,128]{2,0,1:T(8,128)(2,1)S(1)}, u32[]{:S(2)}, u32[]{:S(2)}) collective-permute-start(bf16[128,2,128]{2,0,1:T(8,128)(2,1)S(1)} %get-tuple-element.4), channel_id=1, source_target_pairs={{0,8},{8,16},{16,24},{24,32},{32,40},{40,48},{48,56},{56,64},{64,7... | collective-permute-start | bytes 196616 | tf_op jit(solution)/shard_map/ppermute | solution.py:15
  24.0 8.6 %copy-start.7 = (bf16[512,512]{1,0:T(8,128)(2,1)S(1)}, bf16[512,512]{1,0:T(8,128)(2,1)}, u32[]{:S(2)}) copy-start(bf16[512,512]{1,0:T(8,128)(2,1)} %param.37) | copy-start | bytes 1572868
  26.5 16.5 %copy-start.5 = (f32[8,128]{1,0:T(8,128)S(1)}, f32[8,128]{1,0:T(8,128)}, u32[]{:S(2)}) copy-start(f32[8,128]{1,0:T(8,128)} %param.32) | copy-start | bytes 12292
  27.7 21.7 %copy-start.4 = (f32[1280]{0:T(1024)S(1)}, f32[1280]{0:T(1024)}, u32[]{:S(2)}) copy-start(f32[1280]{0:T(1024)} %param.29) | copy-start | bytes 15364
  27.7 21.6 %all-to-all-start = ((bf16[8,32,1280]{2,1,0:T(8,128)(2,1)}), bf16[8,32,1280]{2,1,0:T(8,128)(2,1)S(1)}, u32[]{:S(2)}, u32[]{:S(2)}) async-start(bf16[8,32,1280]{2,1,0:T(8,128)(2,1)} %bitcast.7), calls=%async_computation | async-start | bytes 1310720 | tf_op jit(solution)/shard_map/all_to_all | solution.py:140
  32.6 31.4 %collective-permute-start.5 = (bf16[512,512]{1,0:T(8,128)(2,1)S(1)}, bf16[512,512]{1,0:T(8,128)(2,1)S(1)}, u32[]{:S(2)}, u32[]{:S(2)}) collective-permute-start(bf16[512,512]{1,0:T(8,128)(2,1)S(1)} %copy-done.7), channel_id=1, source_target_pairs={{0,0},{1,16},{2,32},{3,48},{4,64},{5,80},{6,96},{7,112},{8,8},{9,2... | collective-permute-start | bytes 1572872 | tf_op jit(solution)/shard_map/ppermute | solution.py:204
  50.3 21.2 %copy-start.2 = (bf16[32,1280]{1,0:T(8,128)(2,1)}, bf16[32,1280]{1,0:T(8,128)(2,1)S(1)}, u32[]{:S(2)}) copy-start(bf16[32,1280]{1,0:T(8,128)(2,1)S(1)} %add_convert_fusion.1) | copy-start | bytes 245764
  54.5 12.9 %all-to-all-start.1 = ((bf16[32,8,256]{2,0,1:T(8,128)(2,1)}), bf16[32,8,256]{2,0,1:T(8,128)(2,1)S(1)}, u32[]{:S(2)}, u32[]{:S(2)}) async-start(bf16[32,8,256]{2,0,1:T(8,128)(2,1)} %bitcast.109), calls=%async_computation.1 | async-start | bytes 262144 | tf_op jit(solution)/shard_map/all_to_all | solution.py:164
  71.5 12.3 %copy-start.3 = (s32[512]{0:T(512)S(1)}, s32[512]{0:T(512)}, u32[]{:S(2)}) copy-start(s32[512]{0:T(512)} %param.38) | copy-start | bytes 6148
  71.5 12.3 %copy-start.6 = (s32[512]{0:T(512)S(1)}, s32[512]{0:T(512)}, u32[]{:S(2)}) copy-start(s32[512]{0:T(512)} %param.39) | copy-start | bytes 6148
  71.5 182.5 %all-to-all-start.2 = ((bf16[16,512,512]{1,2,0:T(8,128)(2,1)}), bf16[16,512,512]{1,2,0:T(8,128)(2,1)}, u32[]{:S(2)}, u32[]{:S(2)}) async-start(bf16[16,512,512]{1,2,0:T(8,128)(2,1)} %stack.20), calls=%async_computation.2 | async-start | bytes 16777216 | tf_op jit(solution)/shard_map/all_to_all | solution.py:208
  83.8 138.1 %copy-start.8 = (f32[8192]{0:T(1024)S(1)}, f32[8192]{0:T(1024)}, u32[]{:S(2)}) copy-start(f32[8192]{0:T(1024)} %param.34) | copy-start | bytes 98308
  83.8 138.1 %copy-start.9 = (f32[512]{0:T(512)S(1)}, f32[512]{0:T(512)}, u32[]{:S(2)}) copy-start(f32[512]{0:T(512)} %param.36) | copy-start | bytes 6148
  89.5 104.5 %collective-permute-start.3 = (bf16[256,1,256]{2,0,1:T(8,128)(2,1)S(1)}, bf16[256,1,256]{2,0,1:T(8,128)(2,1)S(1)}, u32[]{:S(2)}, u32[]{:S(2)}) collective-permute-start(bf16[256,1,256]{2,0,1:T(8,128)(2,1)S(1)} %bitcast.118), channel_id=1, source_target_pairs={{8,0},{16,8},{24,16},{32,24},{40,32},{48,40},{56,48},{64,56},{72,6... | collective-permute-start | bytes 393224 | tf_op jit(solution)/shard_map/ppermute | solution.py:18
  92.3 129.6 %collective-permute-start.2 = (bf16[256,1,256]{2,0,1:T(8,128)(2,1)S(1)}, bf16[256,1,256]{2,0,1:T(8,128)(2,1)S(1)}, u32[]{:S(2)}, u32[]{:S(2)}) collective-permute-start(bf16[256,1,256]{2,0,1:T(8,128)(2,1)S(1)} %bitcast.119), channel_id=1, source_target_pairs={{0,8},{8,16},{16,24},{24,32},{32,40},{40,48},{48,56},{56,64},{64,7... | collective-permute-start | bytes 393224 | tf_op jit(solution)/shard_map/ppermute | solution.py:15
  236.9 2.0 collective-permute-start.4
  239.1 14.9 %collective-permute-start.6 = (bf16[2,512,512]{1,2,0:T(8,128)(2,1)S(1)}, bf16[2,512,512]{1,2,0:T(8,128)(2,1)S(1)}, u32[]{:S(2)}, u32[]{:S(2)}) collective-permute-start(bf16[2,512,512]{1,2,0:T(8,128)(2,1)S(1)} %maximum_select_fusion), channel_id=1, source_target_pairs={{0,2},{1,7},{2,4},{3,1},{4,6},{5,3},{6,0},{7,5},{8,10},{9,15},{10,... | collective-permute-start | bytes 3145736 | tf_op jit(solution)/shard_map/ppermute | solution.py:53
  254.0 14.8 %collective-permute-start.7 = (bf16[2,512,512]{1,2,0:T(8,128)(2,1)S(1)}, bf16[2,512,512]{1,2,0:T(8,128)(2,1)S(1)}, u32[]{:S(2)}, u32[]{:S(2)}) collective-permute-start(bf16[2,512,512]{1,2,0:T(8,128)(2,1)S(1)} %collective-permute-done.6), channel_id=1, source_target_pairs={{0,2},{1,7},{2,4},{3,1},{4,6},{5,3},{6,0},{7,5},{8,10},{9,15},{10,... | collective-permute-start | bytes 3145736 | tf_op jit(solution)/shard_map/ppermute | solution.py:54
  258.0 14.8 %collective-permute-start.8 = (bf16[2,512,512]{1,2,0:T(8,128)(2,1)S(1)}, bf16[2,512,512]{1,2,0:T(8,128)(2,1)S(1)}, u32[]{:S(2)}, u32[]{:S(2)}) collective-permute-start(bf16[2,512,512]{1,2,0:T(8,128)(2,1)S(1)} %collective-permute-done.6), channel_id=1, source_target_pairs={{0,1},{1,0},{2,3},{3,2},{4,5},{5,4},{6,7},{7,6},{8,9},{9,8},{10,11... | collective-permute-start | bytes 3145736 | tf_op jit(solution)/shard_map/ppermute | solution.py:55
  270.8 8.1 %copy-start.1 = (bf16[128,1280]{1,0:T(8,128)(2,1)S(1)}, bf16[128,1280]{1,0:T(8,128)(2,1)}, u32[]{:S(2)}) copy-start(bf16[128,1280]{1,0:T(8,128)(2,1)} %param.28) | copy-start | bytes 983044
Sparse Core Ops, SparseCore 0:
  10.1 170.0 all-gather.1
